TPU v7x, 32 devices: a whole 2x2x4 slice. The times are simulated.
32 devices in a mesh: cache: 8 (over z, x), stream: 4 (over y, core).
Axes of the slice: x: 2, y: 2, z: 4, core: 2. Of those that a mesh axis runs over, the one named last changes fastest.
Arguments:
- queries: bfloat16 [2048, 4096], P('cache', 'stream'), may hold values from -12.5 to 12.5
- own_kv: bfloat16 [2048, 1024], P('cache', 'stream'), may hold values from -6 to 6
- passage_store: bfloat16 [128, 512, 1024], P('cache', None, 'stream'), may hold values from -6 to 6
- out_weight: bfloat16 [4096, 8192], P('stream', 'cache'), may hold values from -0.375 to 0.375
- passage_slot: int32 [128], replicated, may hold values from 0 to 127, as said below
- retrieved: int32 [16, 16], P('cache'), may hold values from 0 to 127, as said below
Outputs:
- layer_out: bfloat16 [2048, 8192], P('cache', 'stream')
Inputs may be any that keep to these rules, and one draw needn't show every extreme that they name: `passage_slot`: a permutation. `retrieved`: over the 2 queries of one index of cache all ids are distinct; at most 8 of their slots fall in any one block of 16 consecutive slots, and some block holds exactly 8 of them for every index of cache.
All inputs are finite; a program needn't handle non-finite values.
Results may differ from a plain program's by a relative error of at most 0.015.
Values may be sent and summed in bfloat16 or wider, within the bound.
No kernel may reach another device: no remote copies, remote signals or barrier semaphores. Data moves between devices by JAX's collectives and lax.ppermute only.
A program may use at most 192 MiB of HBM per device.

v0:
```python
import math
import jax
import jax.numpy as jnp
from jax import lax
from jax.sharding import PartitionSpec as P

HD = 128
QLEN = 128
PLEN = 512


def attend_query(query_rows, own_rows, passages):
    kv_count = own_rows.shape[1] // (2 * HD)
    groups = query_rows.shape[1] // (kv_count * HD)
    tokens_here = query_rows.shape[0]
    passage_len = passages.shape[0]
    length = passage_len + tokens_here
    context = jnp.concatenate([passages, own_rows], axis=0).reshape(length, kv_count, 2, HD)
    key_part = context[:, :, 0, :]
    value_part = context[:, :, 1, :]
    query_part = query_rows.reshape(tokens_here, kv_count, groups, HD)
    scores = jnp.einsum(
        "tkgd,lkd->kgtl", query_part, key_part, preferred_element_type=jnp.float32
    ) / math.sqrt(HD)
    position = jnp.arange(length)[None, :] - passage_len
    visible = position <= jnp.arange(tokens_here)[:, None]
    scores = jnp.where(visible, scores, -jnp.inf)
    row_peak = jnp.max(scores, axis=-1, keepdims=True)
    powers = jnp.exp(scores - row_peak)
    totals = jnp.sum(powers, axis=-1)
    soft_weights = powers.astype(jnp.bfloat16)
    weighted = jnp.einsum(
        "kgtl,lkd->tkgd", soft_weights, value_part, preferred_element_type=jnp.float32
    )
    attended = weighted / jnp.transpose(totals, (2, 0, 1))[..., None]
    return attended.reshape(tokens_here, kv_count * groups * HD).astype(jnp.bfloat16)


def shards(queries, own_kv, passage_store, out_weight, passage_slot, retrieved):
    n_cache = lax.axis_size("cache")
    store_count = passage_store.shape[0]
    width_kv = passage_store.shape[2]
    slot_total = passage_slot.shape[0]
    query_count, per_query = retrieved.shape
    wanted_count = query_count * per_query
    capacity = max(2, (2 * wanted_count + n_cache - 1) // n_cache)
    wanted = retrieved.reshape(wanted_count)
    id_match = wanted[:, None] == jnp.arange(slot_total, dtype=jnp.int32)[None, :]
    store_slots = jnp.sum(jnp.where(id_match, passage_slot[None, :], 0), axis=1)
    owners = store_slots // store_count
    local_rows = store_slots % store_count
    places = jnp.arange(wanted_count, dtype=jnp.int32)
    earlier = (owners[None, :] == owners[:, None]) & (places[None, :] < places[:, None])
    order_rank = jnp.sum(earlier, axis=1)
    flat_slot = owners * capacity + order_rank
    slot_match = flat_slot[:, None] == jnp.arange(n_cache * capacity, dtype=jnp.int32)[None, :]
    send_rows = jnp.sum(jnp.where(slot_match, local_rows[:, None], 0), axis=0).reshape(
        n_cache, capacity
    )
    asked_rows = lax.all_to_all(send_rows, "cache", split_axis=0, concat_axis=0, tiled=True)
    outgoing = passage_store[asked_rows]
    arrived = lax.all_to_all(outgoing, "cache", split_axis=0, concat_axis=0, tiled=True)
    picked = arrived.reshape(n_cache * capacity, PLEN, width_kv)[flat_slot]

    def per_query_block(inputs):
        query_rows, own_rows, passages = inputs
        return attend_query(query_rows, own_rows, passages)

    attended = lax.map(
        per_query_block,
        (
            queries.reshape(query_count, QLEN, queries.shape[1]),
            own_kv.reshape(query_count, QLEN, own_kv.shape[1]),
            picked.reshape(query_count, per_query * PLEN, width_kv),
        ),
    )
    attended = attended.reshape(query_count * QLEN, queries.shape[1])
    return project(attended, out_weight)


def project(attended, out_weight):
    n_cache = lax.axis_size("cache")
    n_stream = lax.axis_size("stream")
    rows = attended.shape[0]
    group = n_cache // n_stream
    everyone = lax.all_gather(attended, "cache", axis=0, tiled=True)
    partial_sums = jnp.dot(everyone, out_weight, preferred_element_type=jnp.float32)
    reduced = lax.psum_scatter(
        partial_sums.astype(jnp.bfloat16), "stream", scatter_dimension=0, tiled=True
    )
    me = lax.axis_index("cache")
    width = reduced.shape[1]
    out = jnp.zeros((rows, group * width), reduced.dtype)
    for r in range(group):
        take = (me % group + r) % group
        piece = lax.dynamic_slice_in_dim(reduced, take * rows, rows, axis=0)
        perm = []
        for c in range(n_cache):
            for s in range(n_stream):
                dst_c = s * group + (c % group + r) % group
                dst_s = c // group
                perm.append((c * n_stream + s, dst_c * n_stream + dst_s))
        got = lax.ppermute(piece, ("cache", "stream"), perm)
        put = (me - r) % group
        out = lax.dynamic_update_slice_in_dim(out, got, put * width, axis=1)
    return out


def solution(mesh):
    return jax.shard_map(
        shards,
        mesh=mesh,
        in_specs=(
            P("cache", "stream"),
            P("cache", "stream"),
            P("cache", None, "stream"),
            P("stream", "cache"),
            P(),
            P("cache", None),
        ),
        out_specs=P("cache", "stream"),
        check_vma=False,
    )
```

profile of v0, /device:TPU:4, one launch (start us, length us, event | category | flops | bytes accessed | tf_op | source)
XLA Modules:
  0.0 729.6 jit_solution(13120011358236367580)
XLA Ops:
  6.5 0.9 eq.50
  7.4 0.8 select_reduce_fusion.1
  8.7 12.1 %all_to_all.17 = s32[8,1,8]{2,1,0:T(1,128)S(1)} all-to-all(s32[8,1,8]{2,1,0:T(1,128)S(1)} %bitcast.128), channel_id=1, replica_groups=mesh['cache'=8,'stream'=4] {'cache'}, dimensions={0} | all-to-all | bytes 512 | tf_op jit(solution)/shard_map/all_to_all | solution.py:60
  20.8 9.6 %gather_fusion = bf16[64,512,256]{2,1,0:T(8,128)(2,1)} fusion(bf16[16,512,256]{2,1,0:T(8,128)(2,1)} %param.10, s32[1024]{0:T(1024)S(1)} %pad_clamp_fusion.1), kind=kCustom, calls=%fused_computation | custom fusion | bytes 33554688 | tf_op jit(solution)/shard_map/gather | solution.py:61
  30.4 5.8 all-to-all-start.1
  36.2 361.6 %all-to-all-done.1 = bf16[8,8,512,256]{3,2,1,0:T(8,128)(2,1)} async-done(((bf16[8,8,512,256]{3,2,1,0:T(8,128)(2,1)}), bf16[8,8,512,256]{3,2,1,0:T(8,128)(2,1)}, u32[]{:S(2)}, u32[]{:S(2)}) %all-to-all-start.1) | async-done | bytes 16777248 | tf_op jit(solution)/shard_map/all_to_all | solution.py:62
  397.8 10.9 %gather_fusion.1 = bf16[32,512,256]{2,1,0:T(8,128)(2,1)} fusion(bf16[64,512,256]{2,1,0:T(8,128)(2,1)} %bitcast.19, s32[1024]{0:T(1024)S(1)} %pad_clamp_fusion), kind=kCustom, calls=%fused_computation.1 | custom fusion | bytes 16777344 | tf_op jit(solution)/shard_map/gather | solution.py:63
  408.7 135.2 %while.12 = (s32[]{:T(128)}, bf16[2,128,1024]{2,1,0:T(8,128)(2,1)}, bf16[2,8192,256]{2,1,0:T(8,128)(2,1)}, bf16[2,128,256]{2,1,0:T(8,128)(2,1)S(1)}, bf16[2,128,1024]{2,1,0:T(8,128)(2,1)S(1)}, /*index=5*/s32[]{:T(128)}) while((s32[]{:T(128)}, bf16[2,128,1024]{2,1,0:T(8,128)(2,1)}, bf16[2,8192,256]{2,1,0:T(8,128)(2,1)}, ...), condition=%wide.region_6.7_spmd, body=%wide.region_3.6_spmd.sunk | while | flops 4465645568 | bytes 143283808 | solution.py:69
  408.7 4.4 constant_dynamic-slice_fusion.10
  413.1 6.4 copy.62
  419.6 6.3 copy.63
  426.4 3.8 iota_compare_fusion.5
  430.2 14.9 %fusion.47 = (f32[8,128]{1,0:T(8,128)S(1)}, f32[8320,128,8]{1,0,2:T(8,128)}) fusion(pred[128,8320]{0,1:T(8,128)(4,1)S(1)} %iota_compare_fusion.5, bf16[128,8,128]{0,2,1:T(8,128)(2,1)S(1)} %bitcast.121, bf16[128,1,2,128]{3,0,2,1:T(8,128)(2,1)S(1)} %copy.61, bf16[8192,1,2,128]{3,0,2,1:T(8,128)(2,1)} %copy.63), kind=kOutput, calls=%fused_computation.6.clone.1 | convolution fusion | flops 2210855936 | bytes 39669760 | tf_op jit(solution)/shard_map/while/body/eval_jaxpr/tkgd,lkd->kgtl/dot_general | solution.py:22
  445.0 14.4 %fusion.48 = f32[8,128]{1,0:T(8,128)S(1)} fusion(f32[8320,128,8]{1,0,2:T(8,128)} %get-tuple-element.135, f32[8,128]{1,0:T(8,128)S(1)} %get-tuple-element.136, pred[128,8320]{0,1:T(8,128)(4,1)S(1)} %iota_compare_fusion.5), kind=kLoop, calls=%fused_computation.4.clone.1 | loop fusion | flops 34077696 | bytes 35151872 | tf_op jit(solution)/shard_map/while/body/eval_jaxpr/reduce_sum | solution.py:30
  459.4 16.1 %fusion.49 = bf16[128,1,8,128]{0,3,2,1:T(8,128)(2,1)S(1)} fusion(f32[8320,128,8]{1,0,2:T(8,128)} %get-tuple-element.135, f32[8,128]{1,0:T(8,128)S(1)} %get-tuple-element.136, pred[128,8320]{0,1:T(8,128)(4,1)S(1)} %iota_compare_fusion.5, bf16[8192,1,2,128]{3,0,2,1:T(8,128)(2,1)} %copy.63, bf16[128,1,2,128]{3,0,2,1:T(8,128)(2,1)S(1)} %copy.61, ...), kind=kOutput, calls=%fused_computation.21.clone.1 | convolution fusion | flops 2219638784 | bytes 39673856 | tf_op jit(solution)/shard_map/while/body/eval_jaxpr/kgtl,lkd->tkgd/dot_general | solution.py:32
  475.6 0.7 constant_dynamic-update-slice_fusion.4
  476.3 4.4 constant_dynamic-slice_fusion.10
  480.8 6.4 copy.62
  487.2 6.3 copy.63
  494.0 3.8 iota_compare_fusion.5
  497.8 14.9 %fusion.47 = (f32[8,128]{1,0:T(8,128)S(1)}, f32[8320,128,8]{1,0,2:T(8,128)}) fusion(pred[128,8320]{0,1:T(8,128)(4,1)S(1)} %iota_compare_fusion.5, bf16[128,8,128]{0,2,1:T(8,128)(2,1)S(1)} %bitcast.121, bf16[128,1,2,128]{3,0,2,1:T(8,128)(2,1)S(1)} %copy.61, bf16[8192,1,2,128]{3,0,2,1:T(8,128)(2,1)} %copy.63), kind=kOutput, calls=%fused_computation.6.clone.1 | convolution fusion | flops 2210855936 | bytes 39669760 | tf_op jit(solution)/shard_map/while/body/eval_jaxpr/tkgd,lkd->kgtl/dot_general | solution.py:22
  512.6 14.4 %fusion.48 = f32[8,128]{1,0:T(8,128)S(1)} fusion(f32[8320,128,8]{1,0,2:T(8,128)} %get-tuple-element.135, f32[8,128]{1,0:T(8,128)S(1)} %get-tuple-element.136, pred[128,8320]{0,1:T(8,128)(4,1)S(1)} %iota_compare_fusion.5), kind=kLoop, calls=%fused_computation.4.clone.1 | loop fusion | flops 34077696 | bytes 35151872 | tf_op jit(solution)/shard_map/while/body/eval_jaxpr/reduce_sum | solution.py:30
  527.0 16.1 %fusion.49 = bf16[128,1,8,128]{0,3,2,1:T(8,128)(2,1)S(1)} fusion(f32[8320,128,8]{1,0,2:T(8,128)} %get-tuple-element.135, f32[8,128]{1,0:T(8,128)S(1)} %get-tuple-element.136, pred[128,8320]{0,1:T(8,128)(4,1)S(1)} %iota_compare_fusion.5, bf16[8192,1,2,128]{3,0,2,1:T(8,128)(2,1)} %copy.63, bf16[128,1,2,128]{3,0,2,1:T(8,128)(2,1)S(1)} %copy.61, ...), kind=kOutput, calls=%fused_computation.21.clone.1 | convolution fusion | flops 2219638784 | bytes 39673856 | tf_op jit(solution)/shard_map/while/body/eval_jaxpr/kgtl,lkd->tkgd/dot_general | solution.py:32
  544.2 72.3 %all-gather.2.cloned.1.call-done = bf16[2048,1024]{1,0:T(8,128)(2,1)} async-done(((bf16[256,1024]{1,0:T(8,128)(2,1)}), bf16[2048,1024]{1,0:T(8,128)(2,1)}) %all-gather.2.cloned.1.call-update) | async-done | bytes 4194320 | tf_op jit(solution)/shard_map/all_gather | solution.py:86
  616.5 8.3 %convolution_convert_fusion = bf16[2048,1024]{1,0:T(8,128)(2,1)} fusion(bf16[2048,1024]{1,0:T(8,128)(2,1)} %all-gather.2.cloned.1.call-done, bf16[1024,1024]{1,0:T(8,128)(2,1)S(1)} %copy-done), kind=kOutput, calls=%fused_computation.31 | convolution fusion | flops 4297064448 | bytes 10485760 | tf_op jit(solution)/shard_map/dot_general | solution.py:87
  624.9 41.7 %reduce-scatter.2.cloned.1.call-done = bf16[512,1024]{1,0:T(8,128)(2,1)} async-done(((bf16[2048,1024]{1,0:T(8,128)(2,1)}), bf16[512,1024]{1,0:T(8,128)(2,1)}) %reduce-scatter.2.cloned.1.call-update) | async-done | bytes 1048592 | tf_op jit(solution)/shard_map/reduce_scatter | solution.py:88
  666.7 2.2 constant_dynamic-slice_fusion.3
  668.9 5.5 collective-permute-start
  674.4 1.5 collective-permute-start.1
  675.8 34.2 %collective-permute-done = bf16[256,1024]{1,0:T(8,128)(2,1)S(1)} collective-permute-done((bf16[256,1024]{1,0:T(8,128)(2,1)}, bf16[256,1024]{1,0:T(8,128)(2,1)S(1)}, u32[]{:S(2)}, u32[]{:S(2)}) %collective-permute-start) | collective-permute-done | bytes 524320 | tf_op jit(solution)/shard_map/ppermute | solution.py:103
  710.3 11.6 %collective-permute-done.1 = bf16[256,1024]{1,0:T(8,128)(2,1)S(1)} collective-permute-done((bf16[256,1024]{1,0:T(8,128)(2,1)}, bf16[256,1024]{1,0:T(8,128)(2,1)S(1)}, u32[]{:S(2)}, u32[]{:S(2)}) %collective-permute-start.1) | collective-permute-done | bytes 524320 | tf_op jit(solution)/shard_map/ppermute | solution.py:103
  721.9 0.8 constant_dynamic-update-slice_fusion.2
  (40 shorter events, 2.9 us)
Async XLA Ops:
  6.5 610.0 %copy-start = (bf16[1024,1024]{1,0:T(8,128)(2,1)S(1)}, bf16[1024,1024]{1,0:T(8,128)(2,1)}, u32[]{:S(2)}) copy-start(bf16[1024,1024]{1,0:T(8,128)(2,1)} %param.11) | copy-start | bytes 6291460
  30.4 367.4 %all-to-all-start.1 = ((bf16[8,8,512,256]{3,2,1,0:T(8,128)(2,1)}), bf16[8,8,512,256]{3,2,1,0:T(8,128)(2,1)}, u32[]{:S(2)}, u32[]{:S(2)}) async-start(bf16[8,8,512,256]{3,2,1,0:T(8,128)(2,1)} %bitcast.120), calls=%async_computation.1 | async-start | bytes 33554432 | tf_op jit(solution)/shard_map/all_to_all | solution.py:62
  36.2 580.4 %all-gather.2.cloned.1.call-start = ((), (), s32[]{:S(2)}) async-start(), calls=%async_computation.3 | async-start | bytes 4718592 | tf_op jit(solution)/shard_map/all_gather | solution.py:86
  397.8 10.9 %copy-start.1 = (bf16[256,1024]{1,0:T(8,128)(2,1)S(1)}, bf16[256,1024]{1,0:T(8,128)(2,1)}, u32[]{:S(2)}) copy-start(bf16[256,1024]{1,0:T(8,128)(2,1)} %param.8) | copy-start | bytes 1572868
  397.8 10.9 %copy-start.3 = (bf16[256,256]{1,0:T(8,128)(2,1)S(1)}, bf16[256,256]{1,0:T(8,128)(2,1)}, u32[]{:S(2)}) copy-start(bf16[256,256]{1,0:T(8,128)(2,1)} %param.9) | copy-start | bytes 393220
  544.0 122.7 %reduce-scatter.2.cloned.1.call-start = ((), (), s32[]{:S(2)}) async-start(), calls=%async_computation.4 | async-start | bytes 5242880 | tf_op jit(solution)/shard_map/reduce_scatter | solution.py:88
  668.9 41.2 %collective-permute-start = (bf16[256,1024]{1,0:T(8,128)(2,1)}, bf16[256,1024]{1,0:T(8,128)(2,1)S(1)}, u32[]{:S(2)}, u32[]{:S(2)}) collective-permute-start(bf16[256,1024]{1,0:T(8,128)(2,1)} %get-tuple-element.99), channel_id=1, source_target_pairs={{0,0},{1,8},{2,16},{3,24},{4,4},{5,12},{6,20},{7,28},{8,1},{9,9},{... | collective-permute-start | bytes 1572872 | tf_op jit(solution)/shard_map/ppermute | solution.py:103
  674.4 47.5 %collective-permute-start.1 = (bf16[256,1024]{1,0:T(8,128)(2,1)}, bf16[256,1024]{1,0:T(8,128)(2,1)S(1)}, u32[]{:S(2)}, u32[]{:S(2)}) collective-permute-start(bf16[256,1024]{1,0:T(8,128)(2,1)} %get-tuple-element.98), channel_id=1, source_target_pairs={{0,4},{1,12},{2,20},{3,28},{4,0},{5,8},{6,16},{7,24},{8,5},{9,13},... | collective-permute-start | bytes 1572872 | tf_op jit(solution)/shard_map/ppermute | solution.py:103
  710.2 11.6 %copy-start.2 = (bf16[256,2048]{1,0:T(8,128)(2,1)}, bf16[256,2048]{1,0:T(8,128)(2,1)S(1)}, u32[]{:S(2)}) copy-start(bf16[256,2048]{1,0:T(8,128)(2,1)S(1)} %constant_dynamic-update-slice_fusion.1) | copy-start | bytes 3145732
Sparse Core Ops, SparseCore 0:
  544.1 72.3 all-gather.1
  625.0 41.6 reduce-scatter.1
where the time goes:
time: 731 us; the launch traced here: 730 us
  waiting for transfers between devices  522 us (71%)
  matrix products  70.2 us (10%)
  local copies, waits for them, and re-layouts  61.7 us (8%)
  other arithmetic  37.4 us (5%)
  between operations  13.5 us (2%)
  starting transfers between devices  12.9 us (2%)
  blocking collectives  12.1 us (2%)
    all_to_all x1, waiting for transfers between devices, shards(): lax.all_to_all(outgoing, 'cache', split_axis=0, concat_axis=0, tiled=True)  362 us
    all_gather x1, waiting for transfers between devices, project(): everyone = lax.all_gather(attended, 'cache', axis=0, tiled=True)  72.3 us
    ppermute x2, waiting for transfers between devices, project(): got = lax.ppermute(piece, ('cache', 'stream'), perm)  45.9 us
    reduce_scatter x1, waiting for transfers between devices, project(): lax.psum_scatter(partial_sums.astype(jnp.bfloat16), 'stream', scatter_dim...  41.7 us
    dot_general x2, matrix products, attend_query(): jnp.einsum('kgtl,lkd->tkgd', soft_weights, value_part, preferred_element_...  32.1 us
    dot_general x2, matrix products, attend_query(): jnp.einsum('tkgd,lkd->kgtl', query_part, key_part, preferred_element_type...  29.7 us
    reduce_sum x2, other arithmetic, attend_query(): totals = jnp.sum(powers, axis=-1)  28.7 us
    dynamic_slice x12, local copies, waits for them, and re-layouts, shards(): lax.map(per_query_block, (queries.reshape(query_count, QLEN, queries.shap...  22.3 us
  transfers between devices with their start and end apart: 5, of which 5 were waited for; matrix products, arithmetic and copies ran while one was open for 0% of the time, Pallas kernels for 0%

commit v1 on v0

--- a/solution.py
+++ b/solution.py
@@ -7,6 +7,19 @@
 HD = 128
 QLEN = 128
 PLEN = 512
+
+
+def close_sectors(chunk, axis_k, local):
+    arr_next, ready = (chunk.shape[:axis_k], chunk.shape[axis_k + 1 :])
+    long_array = jnp.moveaxis(chunk.reshape(*arr_next, local, -1, *ready), axis_k, 0)
+    return long_array
+
+
+def launch_the_sectors(point, d0):
+    point = jnp.moveaxis(point, 0, d0)
+    v_now = point.shape
+    new = point.reshape(*v_now[:d0], v_now[d0] * v_now[d0 + 1], *v_now[d0 + 2 :])
+    return new
 
 
 def attend_query(query_rows, own_rows, passages):
@@ -59,7 +72,16 @@
     )
     asked_rows = lax.all_to_all(send_rows, "cache", split_axis=0, concat_axis=0, tiled=True)
     outgoing = passage_store[asked_rows]
-    arrived = lax.all_to_all(outgoing, "cache", split_axis=0, concat_axis=0, tiled=True)
+    far_arr = jax.lax.axis_index("cache")
+    near = jax.lax.axis_size("cache")
+    f_now, placed = (near, far_arr)
+    v1 = close_sectors(outgoing, 0, f_now)
+    inbox = [v1[placed]]
+    for dev_j in tuple(range(1, f_now)):
+        odd = v1[placed ^ dev_j]
+        inbox.append(jax.lax.ppermute(odd, "cache", [(num, num ^ dev_j) for num in range(f_now)]))
+    v1 = jnp.stack(inbox)[placed ^ jnp.arange(f_now)]
+    arrived = launch_the_sectors(v1, 0)
     picked = arrived.reshape(n_cache * capacity, PLEN, width_kv)[flat_slot]
 
     def per_query_block(inputs):

time: 731 us -> 775 us (1.060)
  local copies, waits for them, and re-layouts: 61.7 us -> 106 us
  other arithmetic: 37.4 us -> 51 us
  blocking collectives: 12.1 us -> 0 us
  waiting for transfers between devices: 522 us -> 510 us
  starting transfers between devices: 12.9 us -> 22.6 us
    all_to_all x1, waiting for transfers between devices: 362 us -> 6.3 us  [shards(): lax.all_to_all(send_rows, 'cache', split_axis=0, concat_axis=0, tiled=True)]
    ppermute x0 -> x7, waiting for transfers between devices: none -> 259 us  [shards(): jax.lax.ppermute(odd, 'cache', [(num, num ^ dev_j) for num in range(f_now)])]
    all_gather x1, waiting for transfers between devices: 72.3 us -> 156 us  [project(): everyone = lax.all_gather(attended, 'cache', axis=0, tiled=True)]
    gather x0 -> x3, local copies, waits for them, and re-layouts: none -> 22.3 us  [shards(): v1 = jnp.stack(inbox)[placed ^ jnp.arange(f_now)]]
    unnamed x0 -> x1, other arithmetic: none -> 13.5 us
    all_to_all x1 -> x0, blocking collectives: 12.1 us -> none  [shards(): lax.all_to_all(send_rows, 'cache', split_axis=0, concat_axis=0, tiled=True)]
    squeeze x0 -> x1, local copies, waits for them, and re-layouts: none -> 10.7 us  [shards(): odd = v1[placed ^ dev_j]]
    unnamed x8 -> x15, local copies, waits for them, and re-layouts: 0.02 us -> 10.6 us
  transfers between devices with their start and end apart: 5 -> 12, of which waited for: 5 -> 9; matrix products, arithmetic and copies ran while one was open for 0% -> 1% of each run, Pallas kernels for 0% -> 0%
where the time goes in v1:
time: 775 us; the launch traced here: 773 us
  waiting for transfers between devices  510 us (66%)
  local copies, waits for them, and re-layouts  106 us (14%)
  matrix products  70.2 us (9%)
  other arithmetic  51 us (7%)
  starting transfers between devices  22.6 us (3%)
  between operations  13.6 us (2%)
    ppermute x7, waiting for transfers between devices, shards(): jax.lax.ppermute(odd, 'cache', [(num, num ^ dev_j) for num in range(f_now)])  259 us
    all_gather x1, waiting for transfers between devices, project(): everyone = lax.all_gather(attended, 'cache', axis=0, tiled=True)  156 us
    ppermute x2, waiting for transfers between devices, project(): got = lax.ppermute(piece, ('cache', 'stream'), perm)  45.9 us
    reduce_scatter x1, waiting for transfers between devices, project(): lax.psum_scatter(partial_sums.astype(jnp.bfloat16), 'stream', scatter_dim...  41.7 us
    dot_general x2, matrix products, attend_query(): jnp.einsum('kgtl,lkd->tkgd', soft_weights, value_part, preferred_element_...  32.1 us
    dot_general x2, matrix products, attend_query(): jnp.einsum('tkgd,lkd->kgtl', query_part, key_part, preferred_element_type...  29.8 us
    reduce_sum x2, other arithmetic, attend_query(): totals = jnp.sum(powers, axis=-1)  28.7 us
    gather x3, local copies, waits for them, and re-layouts, shards(): v1 = jnp.stack(inbox)[placed ^ jnp.arange(f_now)]  22.3 us
  transfers between devices with their start and end apart: 12, of which 9 were waited for; matrix products, arithmetic and copies ran while one was open for 1% of the time, Pallas kernels for 0%

profile of v1, /device:TPU:4, one launch (start us, length us, event | category | flops | bytes accessed | tf_op | source)
XLA Modules:
  0.0 773.2 jit_solution(4978737872284901018)
XLA Ops:
  9.3 5.8 all-to-all-start
  15.2 6.3 all-to-all-done
  21.6 9.6 %gather_fusion = bf16[64,512,256]{2,1,0:T(8,128)(2,1)} fusion(bf16[16,512,256]{2,1,0:T(8,128)(2,1)} %param.10, s32[1024]{0:T(1024)S(1)} %pad_clamp_fusion.2), kind=kCustom, calls=%fused_computation | custom fusion | bytes 33554688 | tf_op jit(solution)/shard_map/gather | solution.py:74
  31.2 10.7 %constant_dynamic-slice_fusion.5 = (bf16[1,8,512,256]{3,2,1,0:T(8,128)(2,1)}, bf16[1,8,512,256]{3,2,1,0:T(8,128)(2,1)}, bf16[1,8,512,256]{3,2,1,0:T(8,128)(2,1)}...) fusion(bf16[8,8,512,256]{3,2,1,0:T(8,128)(2,1)} %bitcast.144, ...), kind=kLoop, calls=%fused_computation.59 | loop fusion | bytes 29360156 | tf_op jit(solution)/shard_map/squeeze | solution.py:81
  48.3 39.9 %collective-permute-done = bf16[1,8,512,256]{3,2,1,0:T(8,128)(2,1)} collective-permute-done((bf16[1,8,512,256]{3,2,1,0:T(8,128)(2,1)}, bf16[1,8,512,256]{3,2,1,0:T(8,128)(2,1)}, u32[]{:S(2)}, u32[]{:S(2)}) %collective-permute-start) | collective-permute-done | bytes 2097184 | tf_op jit(solution)/shard_map/ppermute | solution.py:82
  88.9 88.9 %collective-permute-done.1 = bf16[1,8,512,256]{3,2,1,0:T(8,128)(2,1)} collective-permute-done((bf16[1,8,512,256]{3,2,1,0:T(8,128)(2,1)}, bf16[1,8,512,256]{3,2,1,0:T(8,128)(2,1)}, u32[]{:S(2)}, u32[]{:S(2)}) %collective-permute-start.1) | collective-permute-done | bytes 2097184 | tf_op jit(solution)/shard_map/ppermute | solution.py:82
  185.7 35.6 %collective-permute-done.2 = bf16[1,8,512,256]{3,2,1,0:T(8,128)(2,1)} collective-permute-done((bf16[1,8,512,256]{3,2,1,0:T(8,128)(2,1)}, bf16[1,8,512,256]{3,2,1,0:T(8,128)(2,1)}, u32[]{:S(2)}, u32[]{:S(2)}) %collective-permute-start.2) | collective-permute-done | bytes 2097184 | tf_op jit(solution)/shard_map/ppermute | solution.py:82
  224.8 95.0 %collective-permute-done.4 = bf16[1,8,512,256]{3,2,1,0:T(8,128)(2,1)} collective-permute-done((bf16[1,8,512,256]{3,2,1,0:T(8,128)(2,1)}, bf16[1,8,512,256]{3,2,1,0:T(8,128)(2,1)}, u32[]{:S(2)}, u32[]{:S(2)}) %collective-permute-start.4) | collective-permute-done | bytes 2097184 | tf_op jit(solution)/shard_map/ppermute | solution.py:82
  321.9 6.2 slice_bitcast_fusion.1
  328.1 8.1 %gather_fusion.2 = bf16[8,8,256,256]{3,2,1,0:T(8,128)(2,1)} fusion(bf16[8,8,256,256]{3,2,1,0:T(8,128)(2,1)} %get-tuple-element.98, s32[1024]{0:T(1024)S(1)} %get-tuple-element.112), kind=kCustom, calls=%fused_computation.2 | custom fusion | bytes 16777248 | tf_op jit(solution)/shard_map/gather | solution.py:83
  336.2 8.1 %gather_fusion.3 = bf16[8,8,256,256]{3,2,1,0:T(8,128)(2,1)} fusion(bf16[8,8,256,256]{3,2,1,0:T(8,128)(2,1)} %get-tuple-element.99, s32[1024]{0:T(1024)S(1)} %get-tuple-element.112), kind=kCustom, calls=%fused_computation.3 | custom fusion | bytes 16777248 | tf_op jit(solution)/shard_map/gather | solution.py:83
  344.3 13.5 %pad_maximum_fusion.1 = bf16[8,1,8,512,256]{4,3,2,0,1:T(8,128)(2,1)} fusion(bf16[8,1,8,256,256]{4,3,2,0,1:T(8,128)(2,1)} %bitcast.148, bf16[8,1,8,256,256]{4,3,2,0,1:T(8,128)(2,1)} %bitcast.147), kind=kLoop, calls=%fused_computation.33 | loop fusion | flops 33554432 | bytes 33554432
  357.8 10.9 %gather_fusion.1 = bf16[32,512,256]{2,1,0:T(8,128)(2,1)} fusion(bf16[64,512,256]{2,1,0:T(8,128)(2,1)} %bitcast.146, s32[1024]{0:T(1024)S(1)} %get-tuple-element.111), kind=kCustom, calls=%fused_computation.1 | custom fusion | bytes 16777344 | tf_op jit(solution)/shard_map/gather | solution.py:85
  368.7 135.3 %while.12 = (s32[]{:T(128)}, bf16[2,128,1024]{2,1,0:T(8,128)(2,1)}, bf16[2,8192,256]{2,1,0:T(8,128)(2,1)}, bf16[2,128,256]{2,1,0:T(8,128)(2,1)S(1)}, bf16[2,128,1024]{2,1,0:T(8,128)(2,1)S(1)}, /*index=5*/s32[]{:T(128)}) while((s32[]{:T(128)}, bf16[2,128,1024]{2,1,0:T(8,128)(2,1)}, bf16[2,8192,256]{2,1,0:T(8,128)(2,1)}, ...), condition=%wide.region_6.7_spmd, body=%wide.region_3.6_spmd.sunk | while | flops 4465645568 | bytes 143283808 | solution.py:91
  368.7 4.4 constant_dynamic-slice_fusion.17
  373.1 6.4 copy.62
  379.6 6.3 copy.63
  390.2 14.9 %fusion.48 = (f32[8,128]{1,0:T(8,128)S(1)}, f32[8320,128,8]{1,0,2:T(8,128)}) fusion(pred[128,8320]{0,1:T(8,128)(4,1)S(1)} %iota_compare_fusion.5, bf16[128,8,128]{0,2,1:T(8,128)(2,1)S(1)} %bitcast.149, bf16[128,1,2,128]{3,0,2,1:T(8,128)(2,1)S(1)} %copy.61, bf16[8192,1,2,128]{3,0,2,1:T(8,128)(2,1)} %copy.63), kind=kOutput, calls=%fused_computation.8.clone.1 | convolution fusion | flops 2210855936 | bytes 39669760 | tf_op jit(solution)/shard_map/while/body/eval_jaxpr/tkgd,lkd->kgtl/dot_general | solution.py:35
  405.1 14.4 %fusion.49 = f32[8,128]{1,0:T(8,128)S(1)} fusion(f32[8320,128,8]{1,0,2:T(8,128)} %get-tuple-element.146, f32[8,128]{1,0:T(8,128)S(1)} %get-tuple-element.147, pred[128,8320]{0,1:T(8,128)(4,1)S(1)} %iota_compare_fusion.5), kind=kLoop, calls=%fused_computation.6.clone.1 | loop fusion | flops 34077696 | bytes 35151872 | tf_op jit(solution)/shard_map/while/body/eval_jaxpr/reduce_sum | solution.py:43
  419.4 16.1 %fusion.50 = bf16[128,1,8,128]{0,3,2,1:T(8,128)(2,1)S(1)} fusion(f32[8320,128,8]{1,0,2:T(8,128)} %get-tuple-element.146, f32[8,128]{1,0:T(8,128)S(1)} %get-tuple-element.147, pred[128,8320]{0,1:T(8,128)(4,1)S(1)} %iota_compare_fusion.5, bf16[8192,1,2,128]{3,0,2,1:T(8,128)(2,1)} %copy.63, bf16[128,1,2,128]{3,0,2,1:T(8,128)(2,1)S(1)} %copy.61, ...), kind=kOutput, calls=%fused_computation.23.clone.1 | convolution fusion | flops 2219638784 | bytes 39673856 | tf_op jit(solution)/shard_map/while/body/eval_jaxpr/kgtl,lkd->tkgd/dot_general | solution.py:45
  436.4 4.4 constant_dynamic-slice_fusion.17
  440.8 6.4 copy.62
  447.2 6.3 copy.63
  457.8 14.9 %fusion.48 = (f32[8,128]{1,0:T(8,128)S(1)}, f32[8320,128,8]{1,0,2:T(8,128)}) fusion(pred[128,8320]{0,1:T(8,128)(4,1)S(1)} %iota_compare_fusion.5, bf16[128,8,128]{0,2,1:T(8,128)(2,1)S(1)} %bitcast.149, bf16[128,1,2,128]{3,0,2,1:T(8,128)(2,1)S(1)} %copy.61, bf16[8192,1,2,128]{3,0,2,1:T(8,128)(2,1)} %copy.63), kind=kOutput, calls=%fused_computation.8.clone.1 | convolution fusion | flops 2210855936 | bytes 39669760 | tf_op jit(solution)/shard_map/while/body/eval_jaxpr/tkgd,lkd->kgtl/dot_general | solution.py:35
  472.7 14.4 %fusion.49 = f32[8,128]{1,0:T(8,128)S(1)} fusion(f32[8320,128,8]{1,0,2:T(8,128)} %get-tuple-element.146, f32[8,128]{1,0:T(8,128)S(1)} %get-tuple-element.147, pred[128,8320]{0,1:T(8,128)(4,1)S(1)} %iota_compare_fusion.5), kind=kLoop, calls=%fused_computation.6.clone.1 | loop fusion | flops 34077696 | bytes 35151872 | tf_op jit(solution)/shard_map/while/body/eval_jaxpr/reduce_sum | solution.py:43
  487.1 16.1 %fusion.50 = bf16[128,1,8,128]{0,3,2,1:T(8,128)(2,1)S(1)} fusion(f32[8320,128,8]{1,0,2:T(8,128)} %get-tuple-element.146, f32[8,128]{1,0:T(8,128)S(1)} %get-tuple-element.147, pred[128,8320]{0,1:T(8,128)(4,1)S(1)} %iota_compare_fusion.5, bf16[8192,1,2,128]{3,0,2,1:T(8,128)(2,1)} %copy.63, bf16[128,1,2,128]{3,0,2,1:T(8,128)(2,1)S(1)} %copy.61, ...), kind=kOutput, calls=%fused_computation.23.clone.1 | convolution fusion | flops 2219638784 | bytes 39673856 | tf_op jit(solution)/shard_map/while/body/eval_jaxpr/kgtl,lkd->tkgd/dot_general | solution.py:45
  504.1 156.1 %all-gather.2.cloned.1.call-done = bf16[2048,1024]{1,0:T(8,128)(2,1)} async-done(((bf16[256,1024]{1,0:T(8,128)(2,1)}), bf16[2048,1024]{1,0:T(8,128)(2,1)}) %all-gather.2.cloned.1.call-update) | async-done | bytes 4194320 | tf_op jit(solution)/shard_map/all_gather | solution.py:108
  660.2 8.3 %convolution_convert_fusion = bf16[2048,1024]{1,0:T(8,128)(2,1)} fusion(bf16[2048,1024]{1,0:T(8,128)(2,1)} %all-gather.2.cloned.1.call-done, bf16[1024,1024]{1,0:T(8,128)(2,1)S(1)} %copy-done), kind=kOutput, calls=%fused_computation.36 | convolution fusion | flops 4297064448 | bytes 10485760 | tf_op jit(solution)/shard_map/dot_general | solution.py:109
  668.6 41.7 %reduce-scatter.2.cloned.1.call-done = bf16[512,1024]{1,0:T(8,128)(2,1)} async-done(((bf16[2048,1024]{1,0:T(8,128)(2,1)}), bf16[512,1024]{1,0:T(8,128)(2,1)}) %reduce-scatter.2.cloned.1.call-update) | async-done | bytes 1048592 | tf_op jit(solution)/shard_map/reduce_scatter | solution.py:110
  712.6 5.5 collective-permute-start.7
  719.5 34.2 %collective-permute-done.7 = bf16[256,1024]{1,0:T(8,128)(2,1)S(1)} collective-permute-done((bf16[256,1024]{1,0:T(8,128)(2,1)}, bf16[256,1024]{1,0:T(8,128)(2,1)S(1)}, u32[]{:S(2)}, u32[]{:S(2)}) %collective-permute-start.7) | collective-permute-done | bytes 524320 | tf_op jit(solution)/shard_map/ppermute | solution.py:125
  753.9 11.6 %collective-permute-done.8 = bf16[256,1024]{1,0:T(8,128)(2,1)S(1)} collective-permute-done((bf16[256,1024]{1,0:T(8,128)(2,1)}, bf16[256,1024]{1,0:T(8,128)(2,1)S(1)}, u32[]{:S(2)}, u32[]{:S(2)}) %collective-permute-start.8) | collective-permute-done | bytes 524320 | tf_op jit(solution)/shard_map/ppermute | solution.py:125
  (67 shorter events, 38.3 us)
Async XLA Ops:
  6.5 653.7 %copy-start = (bf16[1024,1024]{1,0:T(8,128)(2,1)S(1)}, bf16[1024,1024]{1,0:T(8,128)(2,1)}, u32[]{:S(2)}) copy-start(bf16[1024,1024]{1,0:T(8,128)(2,1)} %param.11) | copy-start | bytes 6291460
  9.3 12.2 %all-to-all-start = ((s32[8,1,8]{2,1,0:T(1,128)}), s32[8,1,8]{2,1,0:T(1,128)S(1)}, u32[]{:S(2)}, u32[]{:S(2)}) async-start(s32[8,1,8]{2,1,0:T(1,128)} %bitcast.16), calls=%async_computation | async-start | bytes 8192 | tf_op jit(solution)/shard_map/all_to_all | solution.py:73
  15.1 645.1 %all-gather.2.cloned.1.call-start = ((), (), s32[]{:S(2)}) async-start(), calls=%async_computation.2 | async-start | bytes 4718592 | tf_op jit(solution)/shard_map/all_gather | solution.py:108
  41.9 46.3 %collective-permute-start = (bf16[1,8,512,256]{3,2,1,0:T(8,128)(2,1)}, bf16[1,8,512,256]{3,2,1,0:T(8,128)(2,1)}, u32[]{:S(2)}, u32[]{:S(2)}) collective-permute-start(bf16[1,8,512,256]{3,2,1,0:T(8,128)(2,1)} %get-tuple-element.106), channel_id=1, source_target_pairs={{0,4},{4,0},{8,12},{12,8},{16,20},{20,16},{24,28},{28,24},{1,5},{5... | collective-permute-start | bytes 6291464 | tf_op jit(solution)/shard_map/ppermute | solution.py:82
  42.4 135.4 %collective-permute-start.1 = (bf16[1,8,512,256]{3,2,1,0:T(8,128)(2,1)}, bf16[1,8,512,256]{3,2,1,0:T(8,128)(2,1)}, u32[]{:S(2)}, u32[]{:S(2)}) collective-permute-start(bf16[1,8,512,256]{3,2,1,0:T(8,128)(2,1)} %get-tuple-element.105), channel_id=1, source_target_pairs={{0,8},{4,12},{8,0},{12,4},{16,24},{20,28},{24,16},{28,20},{1,9},{5... | collective-permute-start | bytes 6291464 | tf_op jit(solution)/shard_map/ppermute | solution.py:82
  43.0 178.3 %collective-permute-start.2 = (bf16[1,8,512,256]{3,2,1,0:T(8,128)(2,1)}, bf16[1,8,512,256]{3,2,1,0:T(8,128)(2,1)}, u32[]{:S(2)}, u32[]{:S(2)}) collective-permute-start(bf16[1,8,512,256]{3,2,1,0:T(8,128)(2,1)} %get-tuple-element.104), channel_id=1, source_target_pairs={{0,12},{4,8},{8,4},{12,0},{16,28},{20,24},{24,20},{28,16},{1,13},{... | collective-permute-start | bytes 6291464 | tf_op jit(solution)/shard_map/ppermute | solution.py:82
  45.4 177.6 %collective-permute-start.3 = (bf16[1,8,512,256]{3,2,1,0:T(8,128)(2,1)}, bf16[1,8,512,256]{3,2,1,0:T(8,128)(2,1)}, u32[]{:S(2)}, u32[]{:S(2)}) collective-permute-start(bf16[1,8,512,256]{3,2,1,0:T(8,128)(2,1)} %get-tuple-element.103), channel_id=1, source_target_pairs={{0,16},{4,20},{8,24},{12,28},{16,0},{20,4},{24,8},{28,12},{1,17},{... | collective-permute-start | bytes 6291464 | tf_op jit(solution)/shard_map/ppermute | solution.py:82
  45.9 273.9 %collective-permute-start.4 = (bf16[1,8,512,256]{3,2,1,0:T(8,128)(2,1)}, bf16[1,8,512,256]{3,2,1,0:T(8,128)(2,1)}, u32[]{:S(2)}, u32[]{:S(2)}) collective-permute-start(bf16[1,8,512,256]{3,2,1,0:T(8,128)(2,1)} %get-tuple-element.102), channel_id=1, source_target_pairs={{0,20},{4,16},{8,28},{12,24},{16,4},{20,0},{24,12},{28,8},{1,21},{... | collective-permute-start | bytes 6291464 | tf_op jit(solution)/shard_map/ppermute | solution.py:82
  88.2 233.4 %collective-permute-start.5 = (bf16[1,8,512,256]{3,2,1,0:T(8,128)(2,1)}, bf16[1,8,512,256]{3,2,1,0:T(8,128)(2,1)S(1)}, u32[]{:S(2)}, u32[]{:S(2)}) collective-permute-start(bf16[1,8,512,256]{3,2,1,0:T(8,128)(2,1)} %get-tuple-element.101), channel_id=1, source_target_pairs={{0,24},{4,28},{8,16},{12,20},{16,8},{20,12},{24,0},{28,4},{1,25},{... | collective-permute-start | bytes 6291464 | tf_op jit(solution)/shard_map/ppermute | solution.py:82
  177.9 143.9 %collective-permute-start.6 = (bf16[1,8,512,256]{3,2,1,0:T(8,128)(2,1)}, bf16[1,8,512,256]{3,2,1,0:T(8,128)(2,1)S(1)}, u32[]{:S(2)}, u32[]{:S(2)}) collective-permute-start(bf16[1,8,512,256]{3,2,1,0:T(8,128)(2,1)} %get-tuple-element.100), channel_id=1, source_target_pairs={{0,28},{4,24},{8,20},{12,16},{16,12},{20,8},{24,4},{28,0},{1,29},{... | collective-permute-start | bytes 6291464 | tf_op jit(solution)/shard_map/ppermute | solution.py:82
  357.8 10.9 %copy-start.1 = (bf16[256,1024]{1,0:T(8,128)(2,1)S(1)}, bf16[256,1024]{1,0:T(8,128)(2,1)}, u32[]{:S(2)}) copy-start(bf16[256,1024]{1,0:T(8,128)(2,1)} %param.8) | copy-start | bytes 1572868
  357.8 10.9 %copy-start.3 = (bf16[256,256]{1,0:T(8,128)(2,1)S(1)}, bf16[256,256]{1,0:T(8,128)(2,1)}, u32[]{:S(2)}) copy-start(bf16[256,256]{1,0:T(8,128)(2,1)} %param.9) | copy-start | bytes 393220
  504.1 206.3 %reduce-scatter.2.cloned.1.call-start = ((), (), s32[]{:S(2)}) async-start(), calls=%async_computation.3 | async-start | bytes 5242880 | tf_op jit(solution)/shard_map/reduce_scatter | solution.py:110
  712.6 41.2 %collective-permute-start.7 = (bf16[256,1024]{1,0:T(8,128)(2,1)}, bf16[256,1024]{1,0:T(8,128)(2,1)S(1)}, u32[]{:S(2)}, u32[]{:S(2)}) collective-permute-start(bf16[256,1024]{1,0:T(8,128)(2,1)} %get-tuple-element.108), channel_id=1, source_target_pairs={{0,0},{1,8},{2,16},{3,24},{4,4},{5,12},{6,20},{7,28},{8,1},{9,9},{... | collective-permute-start | bytes 1572872 | tf_op jit(solution)/shard_map/ppermute | solution.py:125
  718.1 47.5 %collective-permute-start.8 = (bf16[256,1024]{1,0:T(8,128)(2,1)}, bf16[256,1024]{1,0:T(8,128)(2,1)S(1)}, u32[]{:S(2)}, u32[]{:S(2)}) collective-permute-start(bf16[256,1024]{1,0:T(8,128)(2,1)} %get-tuple-element.107), channel_id=1, source_target_pairs={{0,4},{1,12},{2,20},{3,28},{4,0},{5,8},{6,16},{7,24},{8,5},{9,13},... | collective-permute-start | bytes 1572872 | tf_op jit(solution)/shard_map/ppermute | solution.py:125
  753.9 11.6 %copy-start.2 = (bf16[256,2048]{1,0:T(8,128)(2,1)}, bf16[256,2048]{1,0:T(8,128)(2,1)S(1)}, u32[]{:S(2)}) copy-start(bf16[256,2048]{1,0:T(8,128)(2,1)S(1)} %constant_dynamic-update-slice_fusion.1) | copy-start | bytes 3145732
Sparse Core Ops, SparseCore 0:
  504.2 155.9 all-gather.1
  668.7 41.6 reduce-scatter.1
